TPU v7x, 256 devices: a whole 4x4x8 slice. The times are simulated.
256 devices in a mesh: dp: 8 (over x, z_hi), tensor: 32 (over y, z_lo, core).
Axes of the slice: x: 4, y: 4, z: 8 (z_hi: 2, z_lo: 4; z = z_hi * 4 + z_lo), core: 2. Of those that a mesh axis runs over, the one named last changes fastest.
Arguments:
- tokens: bfloat16 [8, 4096, 1280], P('dp', 'tensor'), may hold values from -6 to 6
- segment_ids: int32 [8, 4096], P('dp', 'tensor'), may hold values from 0 to 3, never falling along the last dimension, each value on 1 to 2048 neighbouring positions
- pack_of_group: int32 [32], replicated, may hold values from 0 to 31, each once
- w_qkv: bfloat16 [1280, 1920], replicated, may hold values from -0.11320094 to 0.11320094
- qk_gain: float32 [640], replicated, may hold values from 0.5 to 7
- w_out: bfloat16 [640, 1280], replicated, may hold values from -0.25 to 0.25
- alpha_attn: float32 [1280], replicated, may hold values from 0.05 to 0.6
- w_up: bfloat16 [1280, 5120], P(None, 'dp'), may hold values from -0.15625 to 0.15625
- w_gate: bfloat16 [1280, 5120], P(None, 'dp'), may hold values from -0.15625 to 0.15625
- up_gain: float32 [5120], P('dp'), may hold values from 0.5 to 2
- gate_gain: float32 [5120], P('dp'), may hold values from 0.5 to 2
- w_down: bfloat16 [5120, 1280], P('dp'), may hold values from -0.078125 to 0.078125
- alpha_mlp: float32 [1280], replicated, may hold values from 0.05 to 0.6
- w_vocab: bfloat16 [1280, 32000], P(None, ('dp', 'tensor')), may hold values from -0.15625 to 0.15625
- logit_gain: bfloat16 [32000], P(('dp', 'tensor')), may hold values from 1 to 10
Outputs:
- result_rows: bfloat16 [8, 4096, 1280], P('dp', 'tensor')
- request_norm: float32 [32], replicated
- max_logit: float32 [32], replicated
Inputs may be any that keep to these rules, and one draw needn't show every extreme that they name: `segment_ids`: within a pack the request numbers never fall, every request 0 to 3 has one or more tokens, and one request has exactly 2048 tokens.
All inputs are finite; a program needn't handle non-finite values.
Results may differ from a plain program's by a relative error of at most 0.013.
Values may be sent and summed in bfloat16 or wider, within the bound.
No kernel may reach another device: no remote copies, remote signals or barrier semaphores. Data moves between devices by JAX's collectives and lax.ppermute only.
A program may use at most 128 MiB of HBM per device.

v0:
```python
import math
import jax
import jax.numpy as jnp
from jax import lax
from jax.sharding import PartitionSpec as P

HEADS = 10
HD = 64
REQS = 4
EPSILON = 1e-06
NEGATIVE = -1e30


def normalize(values):
    return values * lax.rsqrt(jnp.mean(values * values, axis=-1, keepdims=True) + EPSILON)


def head_norm(values, qk_gain):
    reshaped = values.reshape(values.shape[0], HEADS, HD)
    return (normalize(reshaped) * qk_gain.reshape(HEADS, HD)).astype(jnp.bfloat16)


def local(
    tokens,
    segment_ids,
    pack_of_group,
    w_qkv,
    qk_gain,
    w_out,
    alpha_attn,
    w_up,
    w_gate,
    up_gain,
    gate_gain,
    w_down,
    alpha_mlp,
    w_vocab,
    logit_gain,
):
    row_count = tokens.shape[1]
    head_width = HEADS * HD
    segments = segment_ids[0]
    tensor_index = lax.axis_index("tensor")
    positions = tensor_index * row_count + jnp.arange(row_count, dtype=jnp.int32)
    request_numbers = jnp.arange(REQS, dtype=jnp.int32)
    start_rows = normalize(tokens[0].astype(jnp.float32)).astype(jnp.bfloat16)
    projected = jnp.dot(start_rows, w_qkv, preferred_element_type=jnp.float32)
    queries = head_norm(projected[:, :head_width], qk_gain)
    key_rows = head_norm(projected[:, head_width : 2 * head_width], qk_gain).reshape(
        row_count, head_width
    )
    value_rows = projected[:, 2 * head_width :].astype(jnp.bfloat16)
    score_scale = 1.0 / math.sqrt(HD)
    offset = jnp.int32(0)
    state_now = (
        jnp.full((HEADS, row_count), NEGATIVE, jnp.float32),
        jnp.zeros((HEADS, row_count), jnp.float32),
        jnp.zeros((HEADS, row_count, HD), jnp.float32),
    )
    key_all = lax.all_gather(key_rows, "tensor", axis=0, tiled=True)
    value_all = lax.all_gather(value_rows, "tensor", axis=0, tiled=True)
    seg_all = lax.all_gather(segments, "tensor", axis=0, tiled=True)
    tally = jnp.sum((seg_all[:, None] == request_numbers[None, :]).astype(jnp.int32), axis=0)
    total_keys = key_all.shape[0]
    step_size = math.gcd(total_keys, 512)
    for begin in range(0, total_keys, step_size):
        key_part = key_all[begin : begin + step_size]
        value_part = value_all[begin : begin + step_size]
        seg_part = seg_all[begin : begin + step_size]
        key_pos = offset + begin + jnp.arange(step_size, dtype=jnp.int32)
        update_running_max, update_weight_sum, update_weighted = state_now
        key_count = key_part.shape[0]
        key_heads = key_part.reshape(key_count, HEADS, HD)
        value_heads = value_part.reshape(key_count, HEADS, HD)
        scores = (
            jnp.einsum("qhd,khd->hqk", queries, key_heads, preferred_element_type=jnp.float32)
            * score_scale
        )
        allowed = (seg_part[None, :] == segments[:, None]) & (
            key_pos[None, :] <= positions[:, None]
        )
        new_max = jnp.maximum(
            update_running_max, jnp.max(jnp.where(allowed[None], scores, NEGATIVE), axis=2)
        )
        weights = jnp.where(allowed[None], jnp.exp(scores - new_max[:, :, None]), 0.0)
        factor = jnp.exp(update_running_max - new_max)
        update_weight_sum = update_weight_sum * factor + jnp.sum(weights, axis=2)
        update_weighted = update_weighted * factor[:, :, None] + jnp.einsum(
            "hqk,khd->hqd",
            weights.astype(jnp.bfloat16),
            value_heads,
            preferred_element_type=jnp.float32,
        )
        state_now = (new_max, update_weight_sum, update_weighted)
    folded, tally = (state_now, tally)
    running_max, weight_sum, weighted = folded
    attended = (
        (weighted / weight_sum[:, :, None])
        .transpose(1, 0, 2)
        .reshape(row_count, head_width)
        .astype(jnp.bfloat16)
    )
    attn_rows = normalize(jnp.dot(attended, w_out, preferred_element_type=jnp.float32))
    residual_in = start_rows.astype(jnp.float32)
    mid_rows = normalize(residual_in + alpha_attn * (attn_rows - residual_in)).astype(jnp.bfloat16)
    received = lax.all_gather(mid_rows, "dp", axis=0, tiled=True)
    up_proj = jnp.dot(received, w_up, preferred_element_type=jnp.float32) * up_gain
    gate_proj = jnp.dot(received, w_gate, preferred_element_type=jnp.float32) * gate_gain
    hidden = (up_proj * jax.nn.silu(gate_proj)).astype(jnp.bfloat16)
    mixed_sum = lax.psum_scatter(
        jnp.dot(hidden, w_down, preferred_element_type=jnp.float32).astype(jnp.bfloat16),
        "dp",
        scatter_dimension=0,
        tiled=True,
    ).astype(jnp.float32)
    mlp_rows = normalize(mixed_sum)
    residual_mid = mid_rows.astype(jnp.float32)
    result_rows = normalize(residual_mid + alpha_mlp * (mlp_rows - residual_mid)).astype(
        jnp.bfloat16
    )
    request_ends = jnp.cumsum(tally) - 1
    same_request = segments[:, None] == request_numbers[None, :]
    row_end = jnp.sum(jnp.where(same_request, request_ends[None, :], 0), axis=1)
    is_last = positions == row_end
    member = same_request.astype(jnp.float32)
    chosen = member * is_last[:, None].astype(jnp.float32)
    result_f32 = result_rows.astype(jnp.float32)
    row_sums = jnp.dot(member.T, result_f32, precision=lax.Precision.HIGHEST)
    last_rows = jnp.dot(chosen.T, result_f32, precision=lax.Precision.HIGHEST)
    counts = jnp.sum(member, axis=0)
    row_sums, last_rows, counts = (
        lax.psum(row_sums.astype(jnp.bfloat16), "tensor").astype(jnp.float32),
        lax.psum(last_rows.astype(jnp.bfloat16), "tensor").astype(jnp.float32),
        lax.psum(counts.astype(jnp.bfloat16), "tensor").astype(jnp.float32),
    )
    request_mean = row_sums / counts[:, None]
    group_norm = jnp.sqrt(jnp.mean(request_mean * request_mean, axis=1))
    slot_count = lax.axis_size("dp") * REQS
    every_last, every_norm = (
        lax.all_gather(last_rows, "dp", axis=0, tiled=True),
        lax.all_gather(group_norm, "dp", axis=0, tiled=True),
    )
    logits = jnp.dot(
        every_last.astype(jnp.bfloat16), w_vocab, preferred_element_type=jnp.float32
    ) * logit_gain.astype(jnp.float32)
    every_max = lax.pmax(jnp.max(logits, axis=1), ("dp", "tensor"))
    placement = (pack_of_group[:, None] == jnp.arange(slot_count, dtype=jnp.int32)[None, :]).astype(
        jnp.float32
    )
    request_norm = jnp.dot(every_norm, placement, precision=lax.Precision.HIGHEST)
    max_logit = jnp.dot(every_max, placement, precision=lax.Precision.HIGHEST)
    return (result_rows[None], request_norm, max_logit)


def solution(mesh):
    return jax.shard_map(
        local,
        mesh=mesh,
        in_specs=(
            P("dp", "tensor", None),
            P("dp", "tensor"),
            P(),
            P(),
            P(),
            P(),
            P(),
            P(None, "dp"),
            P(None, "dp"),
            P("dp"),
            P("dp"),
            P("dp", None),
            P(),
            P(None, ("dp", "tensor")),
            P(("dp", "tensor")),
        ),
        out_specs=(P("dp", "tensor", None), P(), P()),
        check_vma=False,
    )
```

profile of v0, /device:TPU:1, one launch (start us, length us, event | category | flops | bytes accessed | tf_op | source)
XLA Modules:
  0.0 689.7 jit_solution(16697699601182889394)
XLA Ops:
  7.2 1.2 fusion.143
  8.5 3.4 fusion.186
  14.2 46.0 %all-gather = s32[1,4096]{1,0:T(1,128)S(1)} all-gather(s32[1,128]{1,0:T(1,128)S(1)} %copy-done.26), channel_id=2, replica_groups=mesh['dp'=8,'tensor'=32] {'tensor'}, dimensions={1}, use_global_device_ids=true | all-gather | bytes 16896 | tf_op jit(solution)/shard_map/all_gather | solution.py:62
  60.5 1.2 fusion.145
  61.7 19.2 %all-gather.8.cloned.1.call-done = bf16[4096,640]{1,0:T(8,128)(2,1)} async-done(((bf16[128,640]{1,0:T(8,128)(2,1)}), bf16[4096,640]{1,0:T(8,128)(2,1)}) %all-gather.8.cloned.1.call-update) | async-done | bytes 5242896 | tf_op jit(solution)/shard_map/all_gather | solution.py:61
  80.8 4.5 fusion.191
  85.3 2.2 copy.88
  87.5 58.2 %all-gather.6.cloned.1.call-done = bf16[4096,640]{1,0:T(8,128)(2,1)} async-done(((bf16[128,640]{1,0:T(8,128)(2,1)}), bf16[4096,640]{1,0:T(8,128)(2,1)}) %all-gather.6.cloned.1.call-update) | async-done | bytes 5242896 | tf_op jit(solution)/shard_map/all_gather | solution.py:60
  145.7 4.9 fusion.192
  150.6 2.2 copy.77
  152.8 2.2 copy.91
  154.9 2.2 copy.89
  157.1 2.2 copy.87
  159.3 2.2 copy.85
  161.5 2.2 copy.83
  163.7 2.2 copy.81
  165.9 2.2 copy.79
  168.1 2.2 copy.92
  170.3 2.2 copy.90
  172.4 2.2 copy.86
  174.6 2.2 copy.84
  176.8 2.2 copy.82
  179.0 1.1 copy.80
  180.1 1.1 copy.78
  181.2 1.8 select_reduce_fusion.6
  190.2 1.8 fusion.4
  192.0 0.7 fusion.100
  193.1 0.7 fusion.124
  193.9 1.6 fusion.12
  195.5 0.7 fusion.127
  196.6 0.7 fusion.94
  197.3 1.6 fusion
  199.0 0.7 fusion.103
  199.7 1.6 fusion.8
  201.4 0.8 fusion.130
  202.5 0.8 fusion.137
  204.8 1.0 multiply_convert_fusion.2
  206.1 81.0 %all-gather.10.cloned.1.call-done = bf16[1024,1280]{1,0:T(8,128)(2,1)} async-done(((bf16[128,1280]{1,0:T(8,128)(2,1)}), bf16[1024,1280]{1,0:T(8,128)(2,1)}) %all-gather.10.cloned.1.call-update) | async-done | bytes 2621456 | tf_op jit(solution)/shard_map/all_gather | solution.py:106
  287.2 5.9 fusion.194
  293.1 8.4 %convolution_convert_fusion = bf16[1024,1280]{1,0:T(8,128)(2,1)} fusion(bf16[640,1280]{1,0:T(8,128)(2,1)S(1)} %copy-done, f32[1024,640]{1,0:T(8,128)} %fusion.194, bf16[1024,1280]{1,0:T(8,128)(2,1)} %all-gather.10.cloned.1.call-done, bf16[1280,640]{1,0:T(8,128)(2,1)S(1)} %copy-done.27, f32[640]{0:T(1024)S(1)} %copy-done.28, f32[640]{0:T(1024)S(1)} %copy-done.29), kind=kOutput, calls=%fused_computation | convolution fusion | flops 3361996800 | bytes 11146240 | tf_op jit(solution)/shard_map/dot_general | solution.py:111
  304.0 94.9 %reduce-scatter.2.cloned.1.call-done = bf16[128,1280]{1,0:T(8,128)(2,1)} async-done(((bf16[1024,1280]{1,0:T(8,128)(2,1)}), bf16[128,1280]{1,0:T(8,128)(2,1)}) %reduce-scatter.2.cloned.1.call-update) | async-done | bytes 327696 | tf_op jit(solution)/shard_map/reduce_scatter | solution.py:110
  398.9 1.1 fusion.142
  400.1 1.3 multiply_reduce_fusion
  401.4 1.4 multiply_convert_fusion.1
  403.2 130.5 %all-reduce.1 = (bf16[4,1280]{1,0:T(4,128)(2,1)S(1)}, bf16[4]{0:T(256)(128)(2,1)S(1)}, bf16[4,1280]{1,0:T(4,128)(2,1)S(1)}) all-reduce(bf16[4,1280]{1,0:T(4,128)(2,1)S(1)} %convolution_convert_fusion.2, bf16[4]{0:T(256)(128)(2,1)S(1)} %convert_reduce_fusion.1, ...), channel_id=1, replica_groups=mesh['dp'=8,'tensor'=32] {'tensor'}, use_global_device_ids=true, to_apply=%region_24.25 | all-reduce | flops 10244 | bytes 40976 | tf_op jit(solution)/shard_map/psum | solution.py:132
  533.7 37.8 %all-gather.1 = bf16[8,4,1280]{2,1,0:T(4,128)(2,1)S(1)} all-gather(bf16[1,4,1280]{2,1,0:T(4,128)(2,1)S(1)} %bitcast.282), channel_id=1, replica_groups=mesh['dp'=8,'tensor'=32] {'dp'}, dimensions={0}, use_global_device_ids=true | all-gather | bytes 92160 | tf_op jit(solution)/shard_map/all_gather | solution.py:140
  572.1 23.2 %all-reduce = f32[32]{0:T(128)S(1)} all-reduce(f32[32]{0:T(128)S(1)} %sqrt_dynamic-update-slice_fusion), channel_id=1, replica_groups=mesh['dp'=8,'tensor'=32] {'dp'}, use_global_device_ids=true, to_apply=%add | all-reduce | flops 32 | bytes 256
  595.3 86.5 %pmax.7 = f32[32]{0:T(128)S(1)} all-reduce(f32[32]{0:T(128)S(1)} %fusion.133), channel_id=1, replica_groups=mesh['dp'=8,'tensor'=32] {'dp','tensor'}, use_global_device_ids=true, to_apply=%region_33.34 | all-reduce | flops 32 | bytes 256 | tf_op jit(solution)/shard_map/pmax | solution.py:146
  (132 shorter events, 16.5 us)
Async XLA Ops:
  7.2 285.9 %copy-start = (bf16[640,1280]{1,0:T(8,128)(2,1)S(1)}, bf16[640,1280]{1,0:T(8,128)(2,1)}, u32[]{:S(2)}) copy-start(bf16[640,1280]{1,0:T(8,128)(2,1)} %param.26) | copy-start | bytes 4915204
  7.2 73.7 %all-gather.8.cloned.1.call-start = ((), (), s32[]{:S(2)}) async-start(), calls=%async_computation.2 | async-start | bytes 5406720 | tf_op jit(solution)/shard_map/all_gather | solution.py:61
  11.9 1.2 copy-start.25
  12.6 1.6 copy-start.26
  12.6 133.1 %all-gather.6.cloned.1.call-start = ((), (), s32[]{:S(2)}) async-start(), calls=%async_computation.1 | async-start | bytes 5406720 | tf_op jit(solution)/shard_map/all_gather | solution.py:60
  13.9 273.3 %all-gather.10.cloned.1.call-start = ((), (), s32[]{:S(2)}) async-start(), calls=%async_computation.3 | async-start | bytes 2949120 | tf_op jit(solution)/shard_map/all_gather | solution.py:106
  180.1 2.9 copy-start.10
  181.2 1.8 copy-start.21
  183.0 1.1 copy-start.9
  183.0 1.1 copy-start.20
  183.7 1.1 copy-start.8
  184.7 1.1 copy-start.7
  185.5 1.1 copy-start.6
  186.5 1.1 copy-start.5
  187.3 1.1 copy-start.4
  188.3 1.1 copy-start.19
  190.2 1.8 copy-start.18
  192.0 1.1 copy-start.17
  193.8 1.6 copy-start.15
  195.5 1.1 copy-start.16
  197.3 1.6 copy-start.14
  199.7 1.7 copy-start.13
  201.4 1.1 copy-start.12
  202.5 1.4 copy-start.11
  202.5 2.0 copy-start.23
  203.3 1.2 copy-start.1
  205.8 87.3 %copy-start.27 = (bf16[1280,640]{1,0:T(8,128)(2,1)S(1)}, bf16[1280,640]{1,0:T(8,128)(2,1)}, u32[]{:S(2)}) copy-start(bf16[1280,640]{1,0:T(8,128)(2,1)} %param.23) | copy-start | bytes 4915204
  205.8 87.2 %copy-start.28 = (f32[640]{0:T(1024)S(1)}, f32[640]{0:T(1024)}, u32[]{:S(2)}) copy-start(f32[640]{0:T(1024)} %param.25) | copy-start | bytes 7684
  205.8 87.2 %copy-start.29 = (f32[640]{0:T(1024)S(1)}, f32[640]{0:T(1024)}, u32[]{:S(2)}) copy-start(f32[640]{0:T(1024)} %param.24) | copy-start | bytes 7684
  205.9 193.1 %reduce-scatter.2.cloned.1.call-start = ((), (), s32[]{:S(2)}) async-start(), calls=%async_computation.4 | async-start | bytes 2949120 | tf_op jit(solution)/shard_map/reduce_scatter | solution.py:110
  301.5 0.7 copy-start.30
  301.5 0.7 copy-start.32
  301.5 98.5 %copy-start.2 = (bf16[128,1280]{1,0:T(8,128)(2,1)S(1)}, bf16[128,1280]{1,0:T(8,128)(2,1)}, u32[]{:S(2)}) copy-start(bf16[128,1280]{1,0:T(8,128)(2,1)} %multiply_convert_fusion.2) | copy-start | bytes 983044
  301.5 98.5 %copy-start.24 = (f32[1280]{0:T(1024)S(1)}, f32[1280]{0:T(1024)}, u32[]{:S(2)}) copy-start(f32[1280]{0:T(1024)} %param.27) | copy-start | bytes 15364
  301.5 270.3 %copy-start.22 = (bf16[1280,125]{1,0:T(8,128)(2,1)S(1)}, bf16[1280,125]{1,0:T(8,128)(2,1)}, u32[]{:S(2)}) copy-start(bf16[1280,125]{1,0:T(8,128)(2,1)} %param.28) | copy-start | bytes 960004
  301.5 380.2 %copy-start.31 = (s32[32]{0:T(128)S(1)}, s32[32]{0:T(128)}, u32[]{:S(2)}) copy-start(s32[32]{0:T(128)} %param.17) | copy-start | bytes 388
  402.8 280.4 %copy-start.3 = (bf16[128,1280]{1,0:T(8,128)(2,1)}, bf16[128,1280]{1,0:T(8,128)(2,1)S(1)}, u32[]{:S(2)}) copy-start(bf16[128,1280]{1,0:T(8,128)(2,1)S(1)} %multiply_convert_fusion.1) | copy-start | bytes 983044
Sparse Core Ops, SparseCore 0:
  12.7 68.0 all-gather.7
  82.7 62.9 all-gather.5
  205.9 81.1 all-gather.9
  301.7 97.1 reduce-scatter.1
where the time goes:
time: 691 us; the launch traced here: 690 us
  blocking collectives  324 us (47%)
  waiting for transfers between devices  253 us (37%)
  local copies, waits for them, and re-layouts  47.8 us (7%)
  matrix products  33 us (5%)
  other arithmetic  16.1 us (2%)
  between operations  15 us (2%)
    psum x1, blocking collectives, local(): lax.psum(row_sums.astype(jnp.bfloat16), 'tensor').astype(jnp.float32)  131 us
    reduce_scatter x1, waiting for transfers between devices, local(): lax.psum_scatter(jnp.dot(hidden, w_down, preferred_element_type=jnp.float...  94.9 us
    pmax x1, blocking collectives, local(): every_max = lax.pmax(jnp.max(logits, axis=1), ('dp', 'tensor'))  86.5 us
    all_gather x1, waiting for transfers between devices, local(): received = lax.all_gather(mid_rows, 'dp', axis=0, tiled=True)  81 us
    all_gather x1, waiting for transfers between devices, local(): key_all = lax.all_gather(key_rows, 'tensor', axis=0, tiled=True)  58.2 us
    all_gather x1, blocking collectives, local(): seg_all = lax.all_gather(segments, 'tensor', axis=0, tiled=True)  46 us
    all_gather x1, blocking collectives, local(): lax.all_gather(last_rows, 'dp', axis=0, tiled=True)  37.8 us
    unnamed x1, blocking collectives  23.2 us
  transfers between devices with their start and end apart: 4, of which 4 were waited for; matrix products, arithmetic and copies ran while one was open for 2% of the time, Pallas kernels for 0%

commit v1 on v0

--- a/solution.py
+++ b/solution.py
@@ -128,8 +128,9 @@
     row_sums = jnp.dot(member.T, result_f32, precision=lax.Precision.HIGHEST)
     last_rows = jnp.dot(chosen.T, result_f32, precision=lax.Precision.HIGHEST)
     counts = jnp.sum(member, axis=0)
+    _lift_view = lambda x0, axis_id: lax.all_gather(x0, axis_id).sum(axis=0)
     row_sums, last_rows, counts = (
-        lax.psum(row_sums.astype(jnp.bfloat16), "tensor").astype(jnp.float32),
+        _lift_view(row_sums.astype(jnp.bfloat16), "tensor").astype(jnp.float32),
         lax.psum(last_rows.astype(jnp.bfloat16), "tensor").astype(jnp.float32),
         lax.psum(counts.astype(jnp.bfloat16), "tensor").astype(jnp.float32),
     )

time: 691 us -> 732 us (1.059)
  blocking collectives: 324 us -> 364 us
    all_gather x0 -> x1, blocking collectives: none -> 43.3 us  [local(): _lift_view = lambda x0, axis_id: lax.all_gather(x0, axis_id).sum(axis=0)]
  transfers between devices with their start and end apart: 4 -> 4, of which waited for: 4 -> 4; matrix products, arithmetic and copies ran while one was open for 2% -> 1% of each run, Pallas kernels for 0% -> 0%
where the time goes in v1:
time: 732 us; the launch traced here: 730 us
  blocking collectives  364 us (50%)
  waiting for transfers between devices  253 us (35%)
  local copies, waits for them, and re-layouts  47.8 us (7%)
  matrix products  33 us (5%)
  other arithmetic  16.3 us (2%)
  between operations  15 us (2%)
    psum x1, blocking collectives, local(): lax.psum(counts.astype(jnp.bfloat16), 'tensor').astype(jnp.float32)  131 us
    reduce_scatter x1, waiting for transfers between devices, local(): lax.psum_scatter(jnp.dot(hidden, w_down, preferred_element_type=jnp.float...  94.9 us
    pmax x1, blocking collectives, local(): every_max = lax.pmax(jnp.max(logits, axis=1), ('dp', 'tensor'))  82.9 us
    all_gather x1, waiting for transfers between devices, local(): received = lax.all_gather(mid_rows, 'dp', axis=0, tiled=True)  81 us
    all_gather x1, waiting for transfers between devices, local(): key_all = lax.all_gather(key_rows, 'tensor', axis=0, tiled=True)  58.2 us
    all_gather x1, blocking collectives, local(): seg_all = lax.all_gather(segments, 'tensor', axis=0, tiled=True)  46 us
    all_gather x1, blocking collectives, local(): _lift_view = lambda x0, axis_id: lax.all_gather(x0, axis_id).sum(axis=0)  43.3 us
    all_gather x1, blocking collectives, local(): lax.all_gather(last_rows, 'dp', axis=0, tiled=True)  37.7 us
  transfers between devices with their start and end apart: 4, of which 4 were waited for; matrix products, arithmetic and copies ran while one was open for 1% of the time, Pallas kernels for 0%

profile of v1, /device:TPU:1, one launch (start us, length us, event | category | flops | bytes accessed | tf_op | source)
XLA Modules:
  0.0 729.9 jit_solution(922582005389861080)
XLA Ops:
  7.2 1.2 fusion.144
  8.5 3.4 fusion.187
  14.2 46.0 %all-gather = s32[1,4096]{1,0:T(1,128)S(1)} all-gather(s32[1,128]{1,0:T(1,128)S(1)} %copy-done.26), channel_id=2, replica_groups=mesh['dp'=8,'tensor'=32] {'tensor'}, dimensions={1}, use_global_device_ids=true | all-gather | bytes 16896 | tf_op jit(solution)/shard_map/all_gather | solution.py:62
  60.5 1.2 fusion.146
  61.7 19.2 %all-gather.10.cloned.1.call-done = bf16[4096,640]{1,0:T(8,128)(2,1)} async-done(((bf16[128,640]{1,0:T(8,128)(2,1)}), bf16[4096,640]{1,0:T(8,128)(2,1)}) %all-gather.10.cloned.1.call-update) | async-done | bytes 5242896 | tf_op jit(solution)/shard_map/all_gather | solution.py:61
  80.8 4.5 fusion.192
  85.3 2.2 copy.88
  87.5 58.2 %all-gather.8.cloned.1.call-done = bf16[4096,640]{1,0:T(8,128)(2,1)} async-done(((bf16[128,640]{1,0:T(8,128)(2,1)}), bf16[4096,640]{1,0:T(8,128)(2,1)}) %all-gather.8.cloned.1.call-update) | async-done | bytes 5242896 | tf_op jit(solution)/shard_map/all_gather | solution.py:60
  145.7 4.9 fusion.193
  150.6 2.2 copy.77
  152.8 2.2 copy.91
  154.9 2.2 copy.89
  157.1 2.2 copy.87
  159.3 2.2 copy.85
  161.5 2.2 copy.83
  163.7 2.2 copy.81
  165.9 2.2 copy.79
  168.1 2.2 copy.92
  170.3 2.2 copy.90
  172.4 2.2 copy.86
  174.6 2.2 copy.84
  176.8 2.2 copy.82
  179.0 1.1 copy.80
  180.1 1.1 copy.78
  181.2 1.8 select_reduce_fusion.6
  190.2 1.8 fusion.5
  192.0 0.7 fusion.101
  193.1 0.7 fusion.125
  193.9 1.6 fusion.13
  195.5 0.7 fusion.128
  197.3 1.6 fusion.1
  199.0 0.7 fusion.104
  199.7 1.6 fusion.9
  201.4 0.8 fusion.131
  202.5 0.8 fusion.138
  204.8 1.0 multiply_convert_fusion.2
  206.1 81.0 %all-gather.12.cloned.1.call-done = bf16[1024,1280]{1,0:T(8,128)(2,1)} async-done(((bf16[128,1280]{1,0:T(8,128)(2,1)}), bf16[1024,1280]{1,0:T(8,128)(2,1)}) %all-gather.12.cloned.1.call-update) | async-done | bytes 2621456 | tf_op jit(solution)/shard_map/all_gather | solution.py:106
  287.2 5.9 fusion.195
  293.1 8.4 %convolution_convert_fusion = bf16[1024,1280]{1,0:T(8,128)(2,1)} fusion(bf16[640,1280]{1,0:T(8,128)(2,1)S(1)} %copy-done, f32[1024,640]{1,0:T(8,128)} %fusion.195, bf16[1024,1280]{1,0:T(8,128)(2,1)} %all-gather.12.cloned.1.call-done, bf16[1280,640]{1,0:T(8,128)(2,1)S(1)} %copy-done.27, f32[640]{0:T(1024)S(1)} %copy-done.28, f32[640]{0:T(1024)S(1)} %copy-done.29), kind=kOutput, calls=%fused_computation | convolution fusion | flops 3361996800 | bytes 11146240 | tf_op jit(solution)/shard_map/dot_general | solution.py:111
  304.0 94.9 %reduce-scatter.2.cloned.1.call-done = bf16[128,1280]{1,0:T(8,128)(2,1)} async-done(((bf16[1024,1280]{1,0:T(8,128)(2,1)}), bf16[128,1280]{1,0:T(8,128)(2,1)}) %reduce-scatter.2.cloned.1.call-update) | async-done | bytes 327696 | tf_op jit(solution)/shard_map/reduce_scatter | solution.py:110
  398.9 1.1 fusion.143
  400.1 1.3 multiply_reduce_fusion
  401.4 1.4 multiply_convert_fusion.1
  403.2 130.6 %all-reduce.1 = (bf16[4]{0:T(256)(128)(2,1)S(1)}, bf16[4,1280]{1,0:T(4,128)(2,1)S(1)}) all-reduce(bf16[4]{0:T(256)(128)(2,1)S(1)} %convert_reduce_fusion.1, bf16[4,1280]{1,0:T(4,128)(2,1)S(1)} %convolution_convert_fusion.1), channel_id=1, replica_groups=mesh['dp'=8,'tensor'=32] {'tensor'}, use_global_device_ids=true, to_apply=%region_26.27 | all-reduce | flops 5124 | bytes 20496 | tf_op jit(solution)/shard_map/psum | solution.py:135
  533.7 37.7 %all-gather.3 = bf16[8,4,1280]{2,1,0:T(4,128)(2,1)S(1)} all-gather(bf16[1,4,1280]{2,1,0:T(4,128)(2,1)S(1)} %bitcast.284), channel_id=1, replica_groups=mesh['dp'=8,'tensor'=32] {'dp'}, dimensions={0}, use_global_device_ids=true | all-gather | bytes 92160 | tf_op jit(solution)/shard_map/all_gather | solution.py:141
  571.8 82.9 %pmax.7 = f32[32]{0:T(128)S(1)} all-reduce(f32[32]{0:T(128)S(1)} %fusion.134), channel_id=1, replica_groups=mesh['dp'=8,'tensor'=32] {'dp','tensor'}, use_global_device_ids=true, to_apply=%region_33.34 | all-reduce | flops 32 | bytes 256 | tf_op jit(solution)/shard_map/pmax | solution.py:147
  654.7 43.3 %all-gather.2 = bf16[32,4,1280]{2,1,0:T(4,128)(2,1)S(1)} all-gather(bf16[1,4,1280]{2,1,0:T(4,128)(2,1)S(1)} %fusion), channel_id=3, replica_groups=mesh['dp'=8,'tensor'=32] {'tensor'}, dimensions={0}, use_global_device_ids=true | all-gather | bytes 337920 | tf_op jit(solution)/shard_map/all_gather | solution.py:131
  698.4 23.6 %all-reduce = f32[32]{0:T(128)S(1)} all-reduce(f32[32]{0:T(128)S(1)} %sqrt_dynamic-update-slice_fusion), channel_id=1, replica_groups=mesh['dp'=8,'tensor'=32] {'dp'}, use_global_device_ids=true, to_apply=%add | all-reduce | flops 32 | bytes 256
  (134 shorter events, 17.4 us)
Async XLA Ops:
  7.2 285.9 %copy-start = (bf16[640,1280]{1,0:T(8,128)(2,1)S(1)}, bf16[640,1280]{1,0:T(8,128)(2,1)}, u32[]{:S(2)}) copy-start(bf16[640,1280]{1,0:T(8,128)(2,1)} %param.26) | copy-start | bytes 4915204
  7.2 73.7 %all-gather.10.cloned.1.call-start = ((), (), s32[]{:S(2)}) async-start(), calls=%async_computation.2 | async-start | bytes 5406720 | tf_op jit(solution)/shard_map/all_gather | solution.py:61
  11.9 1.2 copy-start.25
  12.6 1.6 copy-start.26
  12.6 133.1 %all-gather.8.cloned.1.call-start = ((), (), s32[]{:S(2)}) async-start(), calls=%async_computation.1 | async-start | bytes 5406720 | tf_op jit(solution)/shard_map/all_gather | solution.py:60
  13.9 273.3 %all-gather.12.cloned.1.call-start = ((), (), s32[]{:S(2)}) async-start(), calls=%async_computation.3 | async-start | bytes 2949120 | tf_op jit(solution)/shard_map/all_gather | solution.py:106
  180.1 2.9 copy-start.10
  181.2 1.8 copy-start.21
  183.0 1.1 copy-start.9
  183.0 1.1 copy-start.20
  183.7 1.1 copy-start.8
  184.7 1.1 copy-start.7
  185.5 1.1 copy-start.6
  186.5 1.1 copy-start.5
  187.3 1.1 copy-start.4
  188.3 1.1 copy-start.19
  190.2 1.8 copy-start.18
  192.0 1.1 copy-start.17
  193.8 1.6 copy-start.15
  195.5 1.1 copy-start.16
  197.3 1.6 copy-start.14
  199.7 1.7 copy-start.13
  201.4 1.1 copy-start.12
  202.5 1.4 copy-start.11
  202.5 2.0 copy-start.23
  203.3 1.2 copy-start.1
  205.8 87.3 %copy-start.27 = (bf16[1280,640]{1,0:T(8,128)(2,1)S(1)}, bf16[1280,640]{1,0:T(8,128)(2,1)}, u32[]{:S(2)}) copy-start(bf16[1280,640]{1,0:T(8,128)(2,1)} %param.23) | copy-start | bytes 4915204
  205.8 87.2 %copy-start.28 = (f32[640]{0:T(1024)S(1)}, f32[640]{0:T(1024)}, u32[]{:S(2)}) copy-start(f32[640]{0:T(1024)} %param.25) | copy-start | bytes 7684
  205.8 87.2 %copy-start.29 = (f32[640]{0:T(1024)S(1)}, f32[640]{0:T(1024)}, u32[]{:S(2)}) copy-start(f32[640]{0:T(1024)} %param.24) | copy-start | bytes 7684
  205.9 193.0 %reduce-scatter.2.cloned.1.call-start = ((), (), s32[]{:S(2)}) async-start(), calls=%async_computation.4 | async-start | bytes 2949120 | tf_op jit(solution)/shard_map/reduce_scatter | solution.py:110
  301.5 0.7 copy-start.30
  301.5 0.7 copy-start.32
  301.5 98.5 %copy-start.2 = (bf16[128,1280]{1,0:T(8,128)(2,1)S(1)}, bf16[128,1280]{1,0:T(8,128)(2,1)}, u32[]{:S(2)}) copy-start(bf16[128,1280]{1,0:T(8,128)(2,1)} %multiply_convert_fusion.2) | copy-start | bytes 983044
  301.5 98.5 %copy-start.24 = (f32[1280]{0:T(1024)S(1)}, f32[1280]{0:T(1024)}, u32[]{:S(2)}) copy-start(f32[1280]{0:T(1024)} %param.27) | copy-start | bytes 15364
  301.5 269.9 %copy-start.22 = (bf16[1280,125]{1,0:T(8,128)(2,1)S(1)}, bf16[1280,125]{1,0:T(8,128)(2,1)}, u32[]{:S(2)}) copy-start(bf16[1280,125]{1,0:T(8,128)(2,1)} %param.28) | copy-start | bytes 960004
  301.6 420.4 %copy-start.31 = (s32[32]{0:T(128)S(1)}, s32[32]{0:T(128)}, u32[]{:S(2)}) copy-start(s32[32]{0:T(128)} %param.17) | copy-start | bytes 388
  402.7 320.7 %copy-start.3 = (bf16[128,1280]{1,0:T(8,128)(2,1)}, bf16[128,1280]{1,0:T(8,128)(2,1)S(1)}, u32[]{:S(2)}) copy-start(bf16[128,1280]{1,0:T(8,128)(2,1)S(1)} %multiply_convert_fusion.1) | copy-start | bytes 983044
Sparse Core Ops, SparseCore 0:
  12.7 68.0 all-gather.9
  82.7 62.9 all-gather.7
  205.9 81.1 all-gather.11
  301.7 97.1 reduce-scatter.1
